TPU v7x, 128 devices: a whole 4x4x4 slice. The times are simulated.
128 devices in a mesh: row: 4 (over y), vocab: 32 (over z, x, core).
Axes of the slice: x: 4, y: 4, z: 4, core: 2. Of those that a mesh axis runs over, the one named last changes fastest.
Arguments:
- tokens: bfloat16 [1280, 7168], P(('row', 'vocab')), may hold values from -60 to 60
- norm_gain: float32 [7168], replicated, may hold values from 0.5 to 1.5
- router: bfloat16 [7168, 32], replicated, may hold values from -0.0625 to 0.0625
- routes: int32 [1280, 8], P(('row', 'vocab')), may hold values from 0 to 31, all different within a row; in each aligned block of 10 rows (0 to 9, 10 to 19, ...) at most 3 rows name the same one
- w_gate: bfloat16 [32, 7168, 1024], P('vocab', None, 'row'), may hold values from -0.0625 to 0.0625
- w_up: bfloat16 [32, 7168, 1024], P('vocab', None, 'row'), may hold values from -0.0625 to 0.0625
- w_down: bfloat16 [32, 1024, 7168], P('vocab', 'row'), may hold values from -0.1875 to 0.1875
- head_gain: float32 [7168], replicated, may hold values from 0.5 to 1.5
- head: bfloat16 [65536, 7168], P(('row', 'vocab')), may hold values from -0.18 to 0.18
- draft_logits: bfloat16 [256, 4, 65536], P(None, None, ('row', 'vocab')), may hold values from -18 to 235
- draft_tokens: int32 [256, 4], replicated, may hold values from 0 to 65535
- reject_pos: int32 [256], replicated, may hold values from 0 to 4
Outputs:
- residual: float32 [256, 65536], P(None, ('row', 'vocab'))
- accept: float32 [256, 4], replicated
Inputs may be any that keep to these rules, and one draw needn't show every extreme that they name: `routes`: each row names 8 different experts. Among the rows of one device no expert is named more than 3 times, and some device's rows name some expert exactly 3 times.
All inputs are finite; a program needn't handle non-finite values.
Results may differ from a plain program's by a relative error of at most 0.012.
Values may be sent and summed in bfloat16 or wider, within the bound.
No kernel may reach another device: no remote copies, remote signals or barrier semaphores. Data moves between devices by JAX's collectives and lax.ppermute only.
A program may use at most 256 MiB of HBM per device.

v0:
```python
import jax
import jax.numpy as jnp
from jax import lax
from jax.sharding import PartitionSpec as P

V = 65536
DRAFTS = 4


def rms_norm(values, gain):
    return values * lax.rsqrt(jnp.mean(values * values, axis=-1, keepdims=True) + 1e-06) * gain


def body(
    tokens,
    norm_gain,
    router,
    routes,
    w_gate,
    w_up,
    w_down,
    head_gain,
    head,
    draft_logits,
    draft_tokens,
    reject_pos,
):
    vocab_count = lax.axis_size("vocab")
    rows_dev = tokens.shape[0]
    model_width = tokens.shape[1]
    top_k = routes.shape[1]
    experts = w_gate.shape[0] * vocab_count
    capacity = min(rows_dev, (rows_dev * top_k + experts - 1) // experts)
    ff_part = w_gate.shape[2]
    resid_in = tokens.astype(jnp.float32)
    normed = rms_norm(resid_in, norm_gain).astype(jnp.bfloat16)
    scores = jax.nn.sigmoid(jnp.dot(normed, router, preferred_element_type=jnp.float32))
    member = routes[:, :, None] == jnp.arange(experts, dtype=jnp.int32)[None, None, :]
    chosen = jnp.any(member, axis=1)
    chosen_int = chosen.astype(jnp.int32)
    picked = chosen.astype(jnp.float32) * scores
    weights = 2.5 * picked / jnp.sum(picked, axis=1, keepdims=True)
    earlier = jnp.cumsum(chosen_int, axis=0) - chosen_int
    slot_ids = jnp.arange(capacity, dtype=jnp.int32)[None, :, None]
    selector = ((earlier.T[:, None, :] == slot_ids) & chosen.T[:, None, :]).astype(jnp.float32)
    send_buffer = jnp.einsum(
        "esr,rd->esd", selector.astype(jnp.bfloat16), normed, preferred_element_type=jnp.float32
    ).astype(jnp.bfloat16)
    gate_w = w_gate[0]
    up_w = w_up[0]
    down_w = w_down[0]
    received = lax.all_to_all(send_buffer, "vocab", split_axis=0, concat_axis=0, tiled=True)
    slot_count = received.shape[1]
    shard_piece = lax.all_gather(received, "row", axis=0, tiled=True)
    flat_rows = shard_piece.reshape(-1, model_width)
    gate_out = jnp.dot(flat_rows, gate_w, preferred_element_type=jnp.float32)
    up_out = jnp.dot(flat_rows, up_w, preferred_element_type=jnp.float32)
    hidden_hidden = (jax.nn.silu(gate_out) * up_out).astype(jnp.bfloat16)
    hidden = hidden_hidden.reshape(shard_piece.shape[0], shard_piece.shape[1], ff_part)
    down_out = jnp.dot(hidden.reshape(-1, ff_part), down_w, preferred_element_type=jnp.float32)
    down_out = down_out.astype(jnp.bfloat16).astype(jnp.float32)
    summed = lax.psum_scatter(
        down_out.reshape(received.shape[0] * lax.axis_size("row"), slot_count, model_width).astype(
            jnp.bfloat16
        ),
        "row",
        scatter_dimension=0,
        tiled=True,
    )
    returned = lax.all_to_all(summed, "vocab", split_axis=0, concat_axis=0, tiled=True)
    combine = selector * weights.T[:, None, :]
    moe_sum = jnp.einsum(
        "esr,esd->rd", combine, returned.astype(jnp.float32), precision=lax.Precision.HIGHEST
    )
    mixed_rows = resid_in + moe_sum
    final_normed = rms_norm(mixed_rows, head_gain).astype(jnp.bfloat16)
    local_vocab = head.shape[0]
    logits = lax.dot_general(
        lax.all_gather(final_normed, ("row", "vocab"), axis=0, tiled=True),
        head,
        (((1,), (1,)), ((), ())),
        preferred_element_type=jnp.float32,
    )
    requests = draft_tokens.shape[0]
    slot_total = DRAFTS + 1
    target_logits = logits.reshape(requests, slot_total, local_vocab)
    draft_vals = draft_logits.astype(jnp.float32)
    offset = lax.axis_index(("row", "vocab")) * local_vocab
    local_ids = draft_tokens - offset
    id_match = jnp.arange(local_vocab, dtype=jnp.int32)[None, None, :] == local_ids[:, :, None]
    pick_target = jnp.sum(jnp.where(id_match, target_logits[:, :DRAFTS], 0.0), axis=-1)
    pick_draft = jnp.sum(jnp.where(id_match, draft_vals, 0.0), axis=-1)
    local_top_target = jnp.max(target_logits, axis=-1)
    local_top_draft = jnp.max(draft_vals, axis=-1)
    top_target, top_draft = lax.pmax((local_top_target, local_top_draft), ("row", "vocab"))
    local_sum_target = jnp.sum(jnp.exp(target_logits - top_target[:, :, None]), axis=-1)
    local_sum_draft = jnp.sum(jnp.exp(draft_vals - top_draft[:, :, None]), axis=-1)
    sum_target, sum_draft, pick_t, pick_d = lax.psum(
        (local_sum_target, local_sum_draft, pick_target, pick_draft), ("row", "vocab")
    )
    target = jnp.exp(target_logits - top_target[:, :, None]) / sum_target[:, :, None]
    draft_prob = jnp.exp(draft_vals - top_draft[:, :, None]) / sum_draft[:, :, None]
    log_target = pick_t - top_target[:, :DRAFTS] - jnp.log(sum_target[:, :DRAFTS])
    log_draft = pick_d - top_draft - jnp.log(sum_draft)
    accept = jnp.exp(jnp.minimum(log_target - log_draft, 0.0))
    position = (jnp.arange(slot_total, dtype=jnp.int32)[None, :] == reject_pos[:, None]).astype(
        jnp.float32
    )
    target_at = jnp.sum(position[:, :, None] * target, axis=1)
    draft_at = jnp.sum(position[:, :DRAFTS, None] * draft_prob, axis=1)
    gap_rows = jnp.maximum(target_at - draft_at, 0.0)
    gap_total = lax.psum(jnp.sum(gap_rows, axis=-1), ("row", "vocab"))
    residual = jnp.sqrt(V * gap_rows / gap_total[:, None])
    return (residual, accept)


def solution(mesh):
    placed = (
        P(("row", "vocab"), None),
        P(),
        P(),
        P(("row", "vocab"), None),
        P("vocab", None, "row"),
        P("vocab", None, "row"),
        P("vocab", "row", None),
        P(),
        P(("row", "vocab"), None),
        P(None, None, ("row", "vocab")),
        P(),
        P(),
    )
    return jax.shard_map(
        body,
        mesh=mesh,
        in_specs=placed,
        out_specs=(P(None, ("row", "vocab")), P()),
        check_vma=False,
    )
```

profile of v0, /device:TPU:1, one launch (start us, length us, event | category | flops | bytes accessed | tf_op | source)
XLA Modules:
  0.0 698.3 jit_solution(13152813386539640018)
XLA Ops:
  7.2 0.8 copy.38
  8.2 1.1 fusion.23
  9.3 1.5 convolution_convert_fusion.1
  10.8 1.2 copy.39
  12.0 34.7 %all_to_all.10 = bf16[32,3,7168]{2,1,0:T(4,128)(2,1)S(1)} all-to-all(bf16[32,3,7168]{2,1,0:T(4,128)(2,1)S(1)} %copy.39), channel_id=1, replica_groups=mesh['row'=4,'vocab'=32] {'vocab'}, dimensions={0} | all-to-all | bytes 2752512 | tf_op jit(solution)/shard_map/all_to_all | solution.py:52
  46.7 1.6 copy.40
  48.6 56.5 %all-gather.4.cloned.1.call-done = bf16[128,3,7168]{2,0,1:T(8,128)(2,1)} async-done(((bf16[32,3,7168]{2,0,1:T(8,128)(2,1)}), bf16[128,3,7168]{2,0,1:T(8,128)(2,1)}) %all-gather.4.cloned.1.call-update) | async-done | bytes 5505040 | tf_op jit(solution)/shard_map/all_gather | solution.py:54
  105.1 10.2 %copy.41 = bf16[128,3,7168]{2,1,0:T(4,128)(2,1)} copy(bf16[128,3,7168]{2,0,1:T(8,128)(2,1)} %all-gather.4.cloned.1.call-done) | data formatting | bytes 11010048 | tf_op jit(solution)/shard_map/all_gather | solution.py:54
  115.3 13.0 %reshape.67 = bf16[384,7168]{1,0:T(8,128)(2,1)} reshape(bf16[128,3,7168]{2,1,0:T(4,128)(2,1)} %copy.41) | data formatting | bytes 11010048 | tf_op jit(solution)/shard_map/reshape | solution.py:55
  128.4 5.4 fusion.4
  133.8 0.9 copy-done.12
  134.7 1.6 fusion.17
  136.8 4.0 convolution_convert_fusion
  140.7 12.3 %convert_element_type.57 = bf16[128,3,7168]{2,1,0:T(4,128)(2,1)} reshape(bf16[384,7168]{1,0:T(8,128)(2,1)} %convolution_convert_fusion) | data formatting | bytes 11010048 | tf_op jit(solution)/shard_map/convert_element_type | solution.py:63
  154.9 142.7 %all-reduce.6.cloned.1.call-done = bf16[128,3,7168]{2,1,0:T(4,128)(2,1)} async-done(((bf16[128,3,7168]{2,1,0:T(4,128)(2,1)}), bf16[128,3,7168]{2,1,0:T(4,128)(2,1)}) %all-reduce.6.cloned.1.call-update) | async-done | bytes 5505040
  297.7 3.5 constant_dynamic-slice_fusion
  301.1 8.0 %all-to-all-start.1 = ((bf16[32,3,7168]{2,1,0:T(4,128)(2,1)}), bf16[32,3,7168]{2,1,0:T(4,128)(2,1)S(1)}, u32[]{:S(2)}, u32[]{:S(2)}) async-start(bf16[32,3,7168]{2,1,0:T(4,128)(2,1)} %constant_dynamic-slice_fusion), calls=%async_computation.1 | async-start | bytes 3670016 | tf_op jit(solution)/shard_map/all_to_all | solution.py:70
  309.4 1.4 select_reduce_fusion
  310.8 24.1 %all-to-all-done.1 = bf16[32,3,7168]{2,1,0:T(4,128)(2,1)S(1)} async-done(((bf16[32,3,7168]{2,1,0:T(4,128)(2,1)}), bf16[32,3,7168]{2,1,0:T(4,128)(2,1)S(1)}, u32[]{:S(2)}, u32[]{:S(2)}) %all-to-all-start.1) | async-done | bytes 1376288 | tf_op jit(solution)/shard_map/all_to_all | solution.py:70
  334.9 2.3 multiply_reduce_fusion.1
  339.5 95.4 %all-gather.6.cloned.1.call-done = bf16[128,10,7168]{2,1,0:T(8,128)(2,1)} async-done(((bf16[1,10,7168]{2,1,0:T(8,128)(2,1)}), bf16[128,10,7168]{2,1,0:T(8,128)(2,1)}) %all-gather.6.cloned.1.call-update) | async-done | bytes 18350096 | tf_op jit(solution)/shard_map/all_gather | solution.py:79
  435.0 28.2 %reshape.70 = bf16[1280,7168]{1,0:T(8,128)(2,1)} reshape(bf16[128,10,7168]{2,1,0:T(8,128)(2,1)} %all-gather.6.cloned.1.call-done) | data formatting | bytes 36700160
  463.2 15.7 %fusion.49 = (f32[1280]{0:T(1024)S(1)}, f32[1280,512]{1,0:T(8,128)S(1)}) fusion(bf16[1280,7168]{1,0:T(8,128)(2,1)} %reshape.70, bf16[512,7168]{1,0:T(8,128)(2,1)} %param.20), kind=kOutput, calls=%fused_computation.71 | convolution fusion | flops 9395895296 | bytes 28316672 | tf_op jit(solution)/shard_map/dot_general | solution.py:78
  479.1 65.7 %all-reduce.3 = (f32[256,5]{1,0:T(8,128)S(1)}, f32[256,4]{1,0:T(8,128)S(1)}) all-reduce(f32[256,5]{1,0:T(8,128)S(1)} %reduce_max.26, bf16[256,4]{1,0:T(8,128)(2,1)S(1)} %reduce_max.27), channel_id=1, replica_groups=mesh['row'=4,'vocab'=32] {'row','vocab'}, use_global_device_ids=true, to_apply=%region_7.8 | all-reduce | flops 2304 | bytes 16384 | tf_op jit(solution)/shard_map/pmax | solution.py:95
  545.0 2.1 reshape.68
  547.2 0.9 exponential_reduce_fusion
  548.3 2.4 fusion.8
  550.6 65.5 %all-reduce.2 = (f32[256,5]{1,0:T(8,128)S(1)}, f32[256,4]{1,0:T(8,128)S(1)}) all-reduce(f32[256,5]{1,0:T(8,128)S(1)} %reduce_sum.96, f32[256,4]{1,0:T(8,128)S(1)} %fusion.8), channel_id=1, replica_groups=mesh['row'=4,'vocab'=32] {'row','vocab'}, use_global_device_ids=true, to_apply=%region_9.10 | all-reduce | flops 2304 | bytes 18432 | tf_op jit(solution)/shard_map/psum | solution.py:98
  616.2 3.8 multiply_reduce_fusion
  620.1 5.6 fusion.10
  625.8 64.1 %all-reduce.1 = (f32[256]{0:T(256)S(1)}, f32[256,4]{1,0:T(8,128)S(1)}, f32[256,4]{1,0:T(8,128)S(1)}) all-reduce(f32[256]{0:T(256)S(1)} %fusion.28, f32[256,4]{1,0:T(8,128)} %get-tuple-element.12, f32[256,4]{1,0:T(8,128)S(1)} %get-tuple-element.10), channel_id=1, replica_groups=mesh['row'=4,'vocab'=32] {'row','vocab'}, use_global_device_ids=true, to_apply=%region_17.18 | all-reduce | flops 2304 | bytes 18432 | tf_op jit(solution)/shard_map/psum | solution.py:112
  690.7 1.0 divide_sqrt_fusion
  (52 shorter events, 6.2 us)
Async XLA Ops:
  7.2 302.2 %copy-start = (bf16[7168,32]{0,1:T(8,128)(2,1)S(1)}, bf16[7168,32]{0,1:T(8,128)(2,1)}, u32[]{:S(2)}) copy-start(bf16[7168,32]{0,1:T(8,128)(2,1)} %param.14) | copy-start | bytes 1376260
  7.2 97.9 %all-gather.4.cloned.1.call-start = ((), (), s32[]{:S(2)}) async-start(), calls=%async_computation.2 | async-start | bytes 6881280 | tf_op jit(solution)/shard_map/all_gather | solution.py:54
  48.4 249.3 %all-reduce.6.cloned.1.call-start = ((), (), s32[]{:S(2)}) async-start(), calls=%async_computation.4 | async-start | bytes 14680064
  128.4 5.4 copy-start.5
  128.4 6.3 copy-start.12
  134.7 2.0 copy-start.6
  153.0 0.7 copy-start.13
  154.9 154.4 %copy-start.8 = (f32[7168]{0:T(1024)S(1)}, f32[7168]{0:T(1024)}, u32[]{:S(2)}) copy-start(f32[7168]{0:T(1024)} %param.13) | copy-start | bytes 86020
  301.1 36.1 %copy-start.9 = (f32[7168]{0:T(1024)S(1)}, f32[7168]{0:T(1024)}, u32[]{:S(2)}) copy-start(f32[7168]{0:T(1024)} %param.19) | copy-start | bytes 86020
  301.1 37.0 %copy-start.10 = (s32[256,4]{0,1:T(4,128)S(1)}, s32[256,4]{0,1:T(4,128)}, u32[]{:S(2)}) copy-start(s32[256,4]{0,1:T(4,128)} %param.22) | copy-start | bytes 12292
  301.1 37.8 %copy-start.3 = (bf16[256,4,512]{2,1,0:T(4,128)(2,1)S(1)}, bf16[256,4,512]{2,1,0:T(4,128)(2,1)}, u32[]{:S(2)}) copy-start(bf16[256,4,512]{2,1,0:T(4,128)(2,1)} %param.21) | copy-start | bytes 3145732
  301.1 38.3 %copy-start.11 = (s32[256]{0:T(256)S(1)}, s32[256]{0:T(256)}, u32[]{:S(2)}) copy-start(s32[256]{0:T(256)} %param.23) | copy-start | bytes 3076
  301.1 33.8 %all-to-all-start.1 = ((bf16[32,3,7168]{2,1,0:T(4,128)(2,1)}), bf16[32,3,7168]{2,1,0:T(4,128)(2,1)S(1)}, u32[]{:S(2)}, u32[]{:S(2)}) async-start(bf16[32,3,7168]{2,1,0:T(4,128)(2,1)} %constant_dynamic-slice_fusion), calls=%async_computation.1 | async-start | bytes 3670016 | tf_op jit(solution)/shard_map/all_to_all | solution.py:70
  309.1 125.9 %all-gather.6.cloned.1.call-start = ((), (), s32[]{:S(2)}) async-start(), calls=%async_computation.3 | async-start | bytes 29589504 | tf_op jit(solution)/shard_map/all_gather | solution.py:79
  548.0 72.0 %copy-start.4 = (bf16[256,4,512]{2,1,0:T(4,128)(2,1)S(1)}, bf16[256,4,512]{2,1,0:T(4,128)(2,1)}, u32[]{:S(2)}) copy-start(bf16[256,4,512]{2,1,0:T(4,128)(2,1)} %param.21) | copy-start | bytes 3145732
  548.0 72.0 %copy-start.7 = (s32[256,4]{1,0:T(8,128)S(1)}, s32[256,4]{1,0:T(8,128)}, u32[]{:S(2)}) copy-start(s32[256,4]{1,0:T(8,128)} %copy.43) | copy-start | bytes 12292
  616.2 3.9 copy-start.2
  620.0 71.7 %copy-start.1 = (bf16[7168,32]{0,1:T(8,128)(2,1)S(1)}, bf16[7168,32]{0,1:T(8,128)(2,1)}, u32[]{:S(2)}) copy-start(bf16[7168,32]{0,1:T(8,128)(2,1)} %param.14) | copy-start | bytes 1376260
Sparse Core Ops, SparseCore 0:
  48.5 56.5 all-gather.3
  153.2 144.4 all-reduce.5
  338.2 96.7 all-gather.5
where the time goes:
time: 700 us; the launch traced here: 698 us
  waiting for transfers between devices  319 us (46%)
  blocking collectives  230 us (33%)
  local copies, waits for them, and re-layouts  77.8 us (11%)
  matrix products  31.9 us (5%)
  other arithmetic  16.7 us (2%)
  between operations  14.7 us (2%)
  starting transfers between devices  8.5 us (1%)
    unnamed x4, waiting for transfers between devices  143 us
    all_gather x1, waiting for transfers between devices, body(): lax.all_gather(final_normed, ('row', 'vocab'), axis=0, tiled=True)  95.4 us
    pmax x1, blocking collectives, body(): lax.pmax((local_top_target, local_top_draft), ('row', 'vocab'))  65.7 us
    psum x1, blocking collectives, body(): lax.psum((local_sum_target, local_sum_draft, pick_target, pick_draft), ('...  65.5 us
    psum x1, blocking collectives, body(): gap_total = lax.psum(jnp.sum(gap_rows, axis=-1), ('row', 'vocab'))  64.1 us
    all_gather x1, waiting for transfers between devices, body(): shard_piece = lax.all_gather(received, 'row', axis=0, tiled=True)  56.5 us
    unnamed x33, local copies, waits for them, and re-layouts  35.8 us
    all_to_all x1, blocking collectives, body(): lax.all_to_all(send_buffer, 'vocab', split_axis=0, concat_axis=0, tiled=T...  34.7 us
  transfers between devices with their start and end apart: 4, of which 4 were waited for; matrix products, arithmetic and copies ran while one was open for 0% of the time, Pallas kernels for 0%

commit v1 on v0

--- a/solution.py
+++ b/solution.py
@@ -51,7 +51,8 @@
     down_w = w_down[0]
     received = lax.all_to_all(send_buffer, "vocab", split_axis=0, concat_axis=0, tiled=True)
     slot_count = received.shape[1]
-    shard_piece = lax.all_gather(received, "row", axis=0, tiled=True)
+    copies = jnp.concatenate([received] * lax.axis_size("row"), axis=0)
+    shard_piece = lax.all_to_all(copies, "row", 0, 0, tiled=True)
     flat_rows = shard_piece.reshape(-1, model_width)
     gate_out = jnp.dot(flat_rows, gate_w, preferred_element_type=jnp.float32)
     up_out = jnp.dot(flat_rows, up_w, preferred_element_type=jnp.float32)

time: 700 us -> 720 us (1.029)
  blocking collectives: 230 us -> 316 us
  waiting for transfers between devices: 319 us -> 259 us
  local copies, waits for them, and re-layouts: 77.8 us -> 65.9 us
    all_to_all x0 -> x1, blocking collectives: none -> 85.6 us  [body(): shard_piece = lax.all_to_all(copies, 'row', 0, 0, tiled=True)]
    all_gather x1 -> x0, waiting for transfers between devices: 56.5 us -> none  [body(): shard_piece = lax.all_gather(received, 'row', axis=0, tiled=True)]
    all_gather x1 -> x0, local copies, waits for them, and re-layouts: 10.2 us -> none  [body(): shard_piece = lax.all_gather(received, 'row', axis=0, tiled=True)]
    unnamed x4 -> x3, waiting for transfers between devices: 143 us -> 139 us
  transfers between devices with their start and end apart: 4 -> 3, of which waited for: 4 -> 3; matrix products, arithmetic and copies ran while one was open for 0% -> 0% of each run, Pallas kernels for 0% -> 0%
where the time goes in v1:
time: 720 us; the launch traced here: 718 us
  blocking collectives  316 us (44%)
  waiting for transfers between devices  259 us (36%)
  local copies, waits for them, and re-layouts  65.9 us (9%)
  matrix products  31.9 us (4%)
  other arithmetic  22.1 us (3%)
  between operations  15 us (2%)
  starting transfers between devices  8.24 us (1%)
    unnamed x3, waiting for transfers between devices  139 us
    all_gather x1, waiting for transfers between devices, body(): lax.all_gather(final_normed, ('row', 'vocab'), axis=0, tiled=True)  95.4 us
    all_to_all x1, blocking collectives, body(): shard_piece = lax.all_to_all(copies, 'row', 0, 0, tiled=True)  85.6 us
    pmax x1, blocking collectives, body(): lax.pmax((local_top_target, local_top_draft), ('row', 'vocab'))  65.7 us
    psum x1, blocking collectives, body(): lax.psum((local_sum_target, local_sum_draft, pick_target, pick_draft), ('...  65.5 us
    psum x1, blocking collectives, body(): gap_total = lax.psum(jnp.sum(gap_rows, axis=-1), ('row', 'vocab'))  64.1 us
    unnamed x33, local copies, waits for them, and re-layouts  35.8 us
    all_to_all x1, blocking collectives, body(): lax.all_to_all(send_buffer, 'vocab', split_axis=0, concat_axis=0, tiled=T...  34.7 us
  transfers between devices with their start and end apart: 3, of which 3 were waited for; matrix products, arithmetic and copies ran while one was open for 0% of the time, Pallas kernels for 0%

profile of v1, /device:TPU:1, one launch (start us, length us, event | category | flops | bytes accessed | tf_op | source)
XLA Modules:
  0.0 717.7 jit_solution(660861492023804209)
XLA Ops:
  7.2 0.8 copy.36
  8.2 1.1 fusion.23
  9.3 1.5 convolution_convert_fusion.1
  10.8 1.2 copy.37
  12.0 34.7 %all_to_all.15 = bf16[32,3,7168]{2,1,0:T(4,128)(2,1)S(1)} all-to-all(bf16[32,3,7168]{2,1,0:T(4,128)(2,1)S(1)} %copy.37), channel_id=1, replica_groups=mesh['row'=4,'vocab'=32] {'vocab'}, dimensions={0} | all-to-all | bytes 2752512 | tf_op jit(solution)/shard_map/all_to_all | solution.py:52
  46.7 5.4 pad_maximum_fusion
  52.2 85.6 %all_to_all.16 = bf16[128,3,7168]{2,1,0:T(4,128)(2,1)} all-to-all(bf16[128,3,7168]{2,1,0:T(4,128)(2,1)S(1)} %pad_maximum_fusion), channel_id=1, replica_groups=mesh['row'=4,'vocab'=32] {'row'}, dimensions={0} | all-to-all | bytes 11010048 | tf_op jit(solution)/shard_map/all_to_all | solution.py:55
  137.8 13.0 %reshape.67 = bf16[384,7168]{1,0:T(8,128)(2,1)} reshape(bf16[128,3,7168]{2,1,0:T(4,128)(2,1)} %all_to_all.16) | data formatting | bytes 11010048 | tf_op jit(solution)/shard_map/reshape | solution.py:56
  150.8 5.4 fusion.4
  156.2 0.9 copy-done.12
  157.1 1.6 fusion.17
  159.2 4.0 convolution_convert_fusion
  163.2 12.3 %convert_element_type.57 = bf16[128,3,7168]{2,1,0:T(4,128)(2,1)} reshape(bf16[384,7168]{1,0:T(8,128)(2,1)} %convolution_convert_fusion) | data formatting | bytes 11010048 | tf_op jit(solution)/shard_map/convert_element_type | solution.py:64
  177.4 139.4 %all-reduce.6.cloned.1.call-done = bf16[128,3,7168]{2,1,0:T(4,128)(2,1)} async-done(((bf16[128,3,7168]{2,1,0:T(4,128)(2,1)}), bf16[128,3,7168]{2,1,0:T(4,128)(2,1)}) %all-reduce.6.cloned.1.call-update) | async-done | bytes 5505040
  316.8 3.5 constant_dynamic-slice_fusion
  320.3 8.0 %all-to-all-start.2 = ((bf16[32,3,7168]{2,1,0:T(4,128)(2,1)}), bf16[32,3,7168]{2,1,0:T(4,128)(2,1)S(1)}, u32[]{:S(2)}, u32[]{:S(2)}) async-start(bf16[32,3,7168]{2,1,0:T(4,128)(2,1)} %constant_dynamic-slice_fusion), calls=%async_computation.2 | async-start | bytes 3670016 | tf_op jit(solution)/shard_map/all_to_all | solution.py:71
  328.5 1.4 select_reduce_fusion
  330.0 24.1 %all-to-all-done.2 = bf16[32,3,7168]{2,1,0:T(4,128)(2,1)S(1)} async-done(((bf16[32,3,7168]{2,1,0:T(4,128)(2,1)}), bf16[32,3,7168]{2,1,0:T(4,128)(2,1)S(1)}, u32[]{:S(2)}, u32[]{:S(2)}) %all-to-all-start.2) | async-done | bytes 1376288 | tf_op jit(solution)/shard_map/all_to_all | solution.py:71
  354.1 2.3 multiply_reduce_fusion.1
  356.4 0.8 fusion.26
  358.7 95.4 %all-gather.3.cloned.1.call-done = bf16[128,10,7168]{2,1,0:T(8,128)(2,1)} async-done(((bf16[1,10,7168]{2,1,0:T(8,128)(2,1)}), bf16[128,10,7168]{2,1,0:T(8,128)(2,1)}) %all-gather.3.cloned.1.call-update) | async-done | bytes 18350096 | tf_op jit(solution)/shard_map/all_gather | solution.py:80
  454.1 28.2 %reshape.70 = bf16[1280,7168]{1,0:T(8,128)(2,1)} reshape(bf16[128,10,7168]{2,1,0:T(8,128)(2,1)} %all-gather.3.cloned.1.call-done) | data formatting | bytes 36700160
  482.4 15.7 %fusion.49 = (f32[1280]{0:T(1024)S(1)}, f32[1280,512]{1,0:T(8,128)S(1)}) fusion(bf16[1280,7168]{1,0:T(8,128)(2,1)} %reshape.70, bf16[512,7168]{1,0:T(8,128)(2,1)} %param.20), kind=kOutput, calls=%fused_computation.72 | convolution fusion | flops 9395895296 | bytes 28316672 | tf_op jit(solution)/shard_map/dot_general | solution.py:79
  498.3 65.7 %all-reduce.3 = (f32[256,5]{1,0:T(8,128)S(1)}, f32[256,4]{1,0:T(8,128)S(1)}) all-reduce(f32[256,5]{1,0:T(8,128)S(1)} %reduce_max.26, bf16[256,4]{1,0:T(8,128)(2,1)S(1)} %reduce_max.27), channel_id=1, replica_groups=mesh['row'=4,'vocab'=32] {'row','vocab'}, use_global_device_ids=true, to_apply=%region_7.8 | all-reduce | flops 2304 | bytes 16384 | tf_op jit(solution)/shard_map/pmax | solution.py:96
  564.2 2.1 reshape.68
  566.3 0.9 exponential_reduce_fusion
  567.4 2.4 fusion.8
  569.8 65.5 %all-reduce.2 = (f32[256,5]{1,0:T(8,128)S(1)}, f32[256,4]{1,0:T(8,128)S(1)}) all-reduce(f32[256,5]{1,0:T(8,128)S(1)} %reduce_sum.96, f32[256,4]{1,0:T(8,128)S(1)} %fusion.8), channel_id=1, replica_groups=mesh['row'=4,'vocab'=32] {'row','vocab'}, use_global_device_ids=true, to_apply=%region_9.10 | all-reduce | flops 2304 | bytes 18432 | tf_op jit(solution)/shard_map/psum | solution.py:99
  635.3 3.8 multiply_reduce_fusion
  639.2 5.6 fusion.10
  644.9 64.1 %all-reduce.1 = (f32[256]{0:T(256)S(1)}, f32[256,4]{1,0:T(8,128)S(1)}, f32[256,4]{1,0:T(8,128)S(1)}) all-reduce(f32[256]{0:T(256)S(1)} %fusion.28, f32[256,4]{1,0:T(8,128)} %get-tuple-element.12, f32[256,4]{1,0:T(8,128)S(1)} %get-tuple-element.10), channel_id=1, replica_groups=mesh['row'=4,'vocab'=32] {'row','vocab'}, use_global_device_ids=true, to_apply=%region_17.18 | all-reduce | flops 2304 | bytes 18432 | tf_op jit(solution)/shard_map/psum | solution.py:113
  709.8 1.0 divide_sqrt_fusion
  (49 shorter events, 5.1 us)
Async XLA Ops:
  7.2 321.3 %copy-start = (bf16[7168,32]{0,1:T(8,128)(2,1)S(1)}, bf16[7168,32]{0,1:T(8,128)(2,1)}, u32[]{:S(2)}) copy-start(bf16[7168,32]{0,1:T(8,128)(2,1)} %param.14) | copy-start | bytes 1376260
  7.2 309.6 %all-reduce.6.cloned.1.call-start = ((), (), s32[]{:S(2)}) async-start(), calls=%async_computation.4 | async-start | bytes 14680064
  150.8 5.4 copy-start.5
  150.8 6.3 copy-start.12
  157.1 2.0 copy-start.6
  175.5 0.7 copy-start.13
  177.4 151.1 %copy-start.8 = (f32[7168]{0:T(1024)S(1)}, f32[7168]{0:T(1024)}, u32[]{:S(2)}) copy-start(f32[7168]{0:T(1024)} %param.13) | copy-start | bytes 86020
  320.3 36.1 %copy-start.9 = (f32[7168]{0:T(1024)S(1)}, f32[7168]{0:T(1024)}, u32[]{:S(2)}) copy-start(f32[7168]{0:T(1024)} %param.19) | copy-start | bytes 86020
  320.3 37.0 %copy-start.10 = (s32[256,4]{0,1:T(4,128)S(1)}, s32[256,4]{0,1:T(4,128)}, u32[]{:S(2)}) copy-start(s32[256,4]{0,1:T(4,128)} %param.22) | copy-start | bytes 12292
  320.3 37.8 %copy-start.3 = (bf16[256,4,512]{2,1,0:T(4,128)(2,1)S(1)}, bf16[256,4,512]{2,1,0:T(4,128)(2,1)}, u32[]{:S(2)}) copy-start(bf16[256,4,512]{2,1,0:T(4,128)(2,1)} %param.21) | copy-start | bytes 3145732
  320.3 38.3 %copy-start.11 = (s32[256]{0:T(256)S(1)}, s32[256]{0:T(256)}, u32[]{:S(2)}) copy-start(s32[256]{0:T(256)} %param.23) | copy-start | bytes 3076
  320.3 33.8 %all-to-all-start.2 = ((bf16[32,3,7168]{2,1,0:T(4,128)(2,1)}), bf16[32,3,7168]{2,1,0:T(4,128)(2,1)S(1)}, u32[]{:S(2)}, u32[]{:S(2)}) async-start(bf16[32,3,7168]{2,1,0:T(4,128)(2,1)} %constant_dynamic-slice_fusion), calls=%async_computation.2 | async-start | bytes 3670016 | tf_op jit(solution)/shard_map/all_to_all | solution.py:71
  328.3 125.9 %all-gather.3.cloned.1.call-start = ((), (), s32[]{:S(2)}) async-start(), calls=%async_computation.3 | async-start | bytes 29589504 | tf_op jit(solution)/shard_map/all_gather | solution.py:80
  567.2 72.0 %copy-start.4 = (bf16[256,4,512]{2,1,0:T(4,128)(2,1)S(1)}, bf16[256,4,512]{2,1,0:T(4,128)(2,1)}, u32[]{:S(2)}) copy-start(bf16[256,4,512]{2,1,0:T(4,128)(2,1)} %param.21) | copy-start | bytes 3145732
  567.2 72.0 %copy-start.7 = (s32[256,4]{1,0:T(8,128)S(1)}, s32[256,4]{1,0:T(8,128)}, u32[]{:S(2)}) copy-start(s32[256,4]{1,0:T(8,128)} %copy.39) | copy-start | bytes 12292
  635.3 3.9 copy-start.2
  639.2 71.7 %copy-start.1 = (bf16[7168,32]{0,1:T(8,128)(2,1)S(1)}, bf16[7168,32]{0,1:T(8,128)(2,1)}, u32[]{:S(2)}) copy-start(bf16[7168,32]{0,1:T(8,128)(2,1)} %param.14) | copy-start | bytes 1376260
Sparse Core Ops, SparseCore 0:
  175.6 141.1 all-reduce.5
  357.4 96.7 all-gather.2
